TPU v7x, 256 devices: a whole 4x4x8 slice. The times are simulated.
256 devices in a mesh: seq: 32 (over x_hi, z, core), tp: 8 (over y, x_lo).
Axes of the slice: x: 4 (x_hi: 2, x_lo: 2; x = x_hi * 2 + x_lo), y: 4, z: 8, core: 2. Of those that a mesh axis runs over, the one named last changes fastest.
Arguments:
- proj: bfloat16 [4096, 3, 8192], P('seq', None, 'tp'), may hold values from -6 to 6
- cotangent: bfloat16 [4096, 8192], P('seq', 'tp'), may hold values from -6 to 6
- out_weight: bfloat16 [8192, 8192], P('seq', 'tp'), may hold values from -0.125 to 0.125
- short_weight: float32 [7, 3, 8192], P(None, None, 'tp'), may hold values from -2 to 2
- long_filter: float32 [4096, 8192], P('seq', 'tp')
Outputs:
- grad_proj: bfloat16 [4096, 3, 8192], P('seq', None, 'tp')
- grad_short: float32 [7, 3, 8192], P(None, None, 'tp')
- grad_filter: float32 [4096, 8192], P('seq', 'tp')
All inputs are finite; a program needn't handle non-finite values.
Results may differ from a plain program's by a relative error of at most 0.025.
Values may be sent and summed in bfloat16 or wider, within the bound.
No kernel may reach another device: no remote copies, remote signals or barrier semaphores. Data moves between devices by JAX's collectives and lax.ppermute only.
A program may use at most 128 MiB of HBM per device.

v0:
```python
import math
import jax
import jax.numpy as jnp
from jax import lax
from jax.sharding import PartitionSpec as P

highest = lax.Precision.HIGHEST


def shifted(value, axis, by):
    devices = lax.axis_size(axis)
    pairs = [(i, i + by) for i in range(devices) if 0 <= i + by < devices]
    return lax.ppermute(value, axis, pairs)


def angle_tables(row_count, col_count, modulus):
    row_index = jnp.arange(row_count, dtype=jnp.int32)[:, None]
    col_index = jnp.arange(col_count, dtype=jnp.int32)[None, :]
    phase = (row_index * col_index % modulus).astype(jnp.float32) * (2.0 * math.pi / modulus)
    return (jnp.cos(phase), jnp.sin(phase))


def split_length(length):
    whole_len = 2 * length
    ceiling = 1 << whole_len.bit_length() // 2 - 1
    first_len = 2 * math.gcd(length, ceiling)
    return (first_len, whole_len // first_len)


def spectrum(columns):
    length, channels = columns.shape
    first_len, second_len = split_length(length)
    lower_half = first_len // 2
    whole_len = first_len * second_len
    values = columns.astype(jnp.float32).reshape(lower_half, second_len * channels)
    cos_first, sin_first = angle_tables(first_len, lower_half, first_len)
    real_one = jnp.dot(cos_first, values, precision=highest).reshape(
        first_len, second_len, channels
    )
    imag_one = -jnp.dot(sin_first, values, precision=highest).reshape(
        first_len, second_len, channels
    )
    twist_cos, twist_sin = angle_tables(first_len, second_len, whole_len)
    twist_cos = twist_cos[:, :, None]
    twist_sin = twist_sin[:, :, None]
    real_two = real_one * twist_cos + imag_one * twist_sin
    imag_two = imag_one * twist_cos - real_one * twist_sin
    cos_second, sin_second = angle_tables(second_len, second_len, second_len)
    real_out = jnp.einsum("amc,ml->alc", real_two, cos_second, precision=highest) + jnp.einsum(
        "amc,ml->alc", imag_two, sin_second, precision=highest
    )
    imag_out = jnp.einsum("amc,ml->alc", imag_two, cos_second, precision=highest) - jnp.einsum(
        "amc,ml->alc", real_two, sin_second, precision=highest
    )
    return (real_out, imag_out)


def signal(real_in, imag_in):
    first_len, second_len, channels = real_in.shape
    lower_half = first_len // 2
    whole_len = first_len * second_len
    cos_second, sin_second = angle_tables(second_len, second_len, second_len)
    real_one = jnp.einsum("alc,lm->amc", real_in, cos_second, precision=highest) - jnp.einsum(
        "alc,lm->amc", imag_in, sin_second, precision=highest
    )
    imag_one = jnp.einsum("alc,lm->amc", real_in, sin_second, precision=highest) + jnp.einsum(
        "alc,lm->amc", imag_in, cos_second, precision=highest
    )
    twist_cos, twist_sin = angle_tables(first_len, second_len, whole_len)
    twist_cos = twist_cos[:, :, None]
    twist_sin = twist_sin[:, :, None]
    real_two = real_one * twist_cos - imag_one * twist_sin
    imag_two = real_one * twist_sin + imag_one * twist_cos
    cos_first, sin_first = angle_tables(lower_half, first_len, first_len)
    merged = jnp.dot(
        cos_first, real_two.reshape(first_len, second_len * channels), precision=highest
    ) - jnp.dot(sin_first, imag_two.reshape(first_len, second_len * channels), precision=highest)
    return merged.reshape(lower_half * second_len, channels) / whole_len


def complex_product(left_real, left_imag, right_real, right_imag):
    return (
        left_real * right_real - left_imag * right_imag,
        left_real * right_imag + left_imag * right_real,
    )


def conj_product(left_real, left_imag, right_real, right_imag):
    return (
        left_real * right_real + left_imag * right_imag,
        left_imag * right_real - left_real * right_imag,
    )


def times_bf16(left_array, right_array):
    return (left_array.astype(jnp.float32) * right_array.astype(jnp.float32)).astype(jnp.bfloat16)


def body(proj, cotangent, out_weight, short_weight, long_filter):
    tok_rows = proj.shape[0]
    channels = proj.shape[2]
    taps_count = short_weight.shape[0]
    rim_rows = taps_count - 1
    partial_value = lax.dot_general(
        cotangent,
        lax.all_gather(out_weight, "seq", axis=0, tiled=True),
        (((1,), (1,)), ((), ())),
        preferred_element_type=jnp.float32,
    )
    grad_out = lax.psum_scatter(
        partial_value.astype(jnp.bfloat16), "tp", scatter_dimension=1, tiled=True
    )
    lower_rows = shifted(proj[tok_rows - rim_rows :], "seq", 1)
    extended = jnp.concatenate([lower_rows, proj], axis=0)
    primed = short_weight[0] * extended[rim_rows : rim_rows + tok_rows]
    for offset in range(1, taps_count):
        primed = (
            primed
            + short_weight[offset] * extended[rim_rows - offset : rim_rows - offset + tok_rows]
        )
    primed = primed.astype(jnp.bfloat16)
    query_conv = primed[:, 0]
    keys_conv = primed[:, 1]
    value_conv = primed[:, 2]
    gated_input = times_bf16(keys_conv, value_conv)
    filter_cols = lax.all_to_all(
        long_filter.astype(jnp.bfloat16), "seq", split_axis=1, concat_axis=0, tiled=True
    ).astype(long_filter.dtype)
    filter_real, filter_imag = spectrum(filter_cols)
    gated_cols = lax.all_to_all(gated_input, "seq", split_axis=1, concat_axis=0, tiled=True)
    gated_real, gated_imag = spectrum(gated_cols)
    conv_cols = signal(*complex_product(gated_real, gated_imag, filter_real, filter_imag)).astype(
        jnp.bfloat16
    )
    conv_out = lax.all_to_all(conv_cols, "seq", split_axis=0, concat_axis=1, tiled=True)
    grad_query = times_bf16(grad_out, conv_out)
    grad_conv = times_bf16(grad_out, query_conv)
    grad_cols = lax.all_to_all(grad_conv, "seq", split_axis=1, concat_axis=0, tiled=True)
    grad_real, grad_imag = spectrum(grad_cols)
    gated_grad_cols = signal(*conj_product(grad_real, grad_imag, filter_real, filter_imag)).astype(
        jnp.bfloat16
    )
    filter_grad_cols = signal(*conj_product(grad_real, grad_imag, gated_real, gated_imag))
    gated_grad = lax.all_to_all(gated_grad_cols, "seq", split_axis=0, concat_axis=1, tiled=True)
    grad_filter = lax.all_to_all(
        filter_grad_cols.astype(jnp.bfloat16), "seq", split_axis=0, concat_axis=1, tiled=True
    ).astype(filter_grad_cols.dtype)
    grad_keys = times_bf16(gated_grad, value_conv)
    grad_value = times_bf16(gated_grad, keys_conv)
    grad_primed = jnp.stack([grad_query, grad_keys, grad_value], axis=1)
    next_rows = shifted(grad_primed[:rim_rows], "seq", -1)
    trailing = jnp.concatenate([grad_primed, next_rows], axis=0)
    grad_sum = short_weight[0] * trailing[0:tok_rows]
    for offset in range(1, taps_count):
        grad_sum = grad_sum + short_weight[offset] * trailing[offset : offset + tok_rows]
    grad_proj = grad_sum.astype(jnp.bfloat16)
    grad_wide = grad_primed.astype(jnp.float32)
    local_short = jnp.stack(
        [
            jnp.sum(
                grad_wide
                * extended[rim_rows - offset : rim_rows - offset + tok_rows].astype(jnp.float32),
                axis=0,
            )
            for offset in range(taps_count)
        ]
    )
    short_shape = local_short.shape
    grad_short = lax.psum(local_short.reshape(-1, channels), "seq").reshape(short_shape)
    return (grad_proj, grad_short, grad_filter)


def solution(mesh):
    in_specs = (
        P("seq", None, "tp"),
        P("seq", "tp"),
        P("seq", "tp"),
        P(None, None, "tp"),
        P("seq", "tp"),
    )
    out_specs = (P("seq", None, "tp"), P(None, None, "tp"), P("seq", "tp"))
    return jax.shard_map(body, mesh=mesh, in_specs=in_specs, out_specs=out_specs, check_vma=False)
```

profile of v0, /device:TPU:2, one launch (start us, length us, event | category | flops | bytes accessed | tf_op | source)
XLA Modules:
  0.0 583.1 jit_solution(17212374280899392005)
XLA Ops:
  8.7 1.7 collective-permute-start
  10.5 1.9 copy.45
  12.4 11.3 %all-to-all-start.1 = ((bf16[128,32,32]{0,2,1:T(8,128)(2,1)}), bf16[128,32,32]{0,2,1:T(8,128)(2,1)S(1)}, u32[]{:S(2)}, u32[]{:S(2)}) async-start(bf16[128,32,32]{0,2,1:T(8,128)(2,1)} %bitcast.8), calls=%async_computation.2 | async-start | bytes 524288 | tf_op jit(solution)/shard_map/all_to_all | solution.py:126
  23.9 128.3 %all-gather.2.cloned.1.call-done = bf16[8192,1024]{1,0:T(8,128)(2,1)} async-done(((bf16[256,1024]{1,0:T(8,128)(2,1)}), bf16[8192,1024]{1,0:T(8,128)(2,1)}) %all-gather.2.cloned.1.call-update) | async-done | bytes 16777232 | tf_op jit(solution)/shard_map/all_gather | solution.py:106
  152.2 12.7 %convolution_convert_fusion = bf16[128,8192]{1,0:T(8,128)(2,1)} fusion(bf16[128,1024]{1,0:T(8,128)(2,1)S(1)} %copy-done, bf16[8192,1024]{1,0:T(8,128)(2,1)} %all-gather.2.cloned.1.call-done), kind=kOutput, calls=%fused_computation | convolution fusion | flops 2148532224 | bytes 19136512 | tf_op jit(solution)/shard_map/dot_general | solution.py:104
  165.2 0.9 copy-done.7
  166.1 1.5 fusion.12
  168.5 5.8 all-to-all-start
  174.8 1.1 reshape.149
  177.7 1.2 fusion.73
  178.8 2.1 convolution_subtract_fusion.7
  181.0 1.2 fusion.72
  182.1 2.2 convolution_add_fusion.4
  184.3 4.6 all-to-all-done
  189.4 1.1 reshape.148
  192.2 1.6 fusion.71
  193.8 2.2 convolution_subtract_fusion.8
  196.0 22.9 %reduce-scatter.2.cloned.1.call-done = bf16[128,1024]{1,0:T(8,128)(2,1)} async-done(((bf16[128,8192]{1,0:T(8,128)(2,1)}), bf16[128,1024]{1,0:T(8,128)(2,1)}) %reduce-scatter.2.cloned.1.call-update) | async-done | bytes 262160 | tf_op jit(solution)/shard_map/reduce_scatter | solution.py:110
  218.9 1.0 fusion.57
  220.8 9.2 %all-to-all-start.3 = ((bf16[128,32,32]{0,2,1:T(8,128)(2,1)}), bf16[128,32,32]{0,2,1:T(8,128)(2,1)S(1)}, u32[]{:S(2)}, u32[]{:S(2)}) async-start(bf16[128,32,32]{0,2,1:T(8,128)(2,1)} %bitcast.22), calls=%async_computation.4 | async-start | bytes 524288 | tf_op jit(solution)/shard_map/all_to_all | solution.py:138
  230.0 1.2 fusion.70
  231.1 2.1 convolution_add_fusion.5
  233.3 11.4 %all-to-all-done.3 = bf16[128,32,32]{0,2,1:T(8,128)(2,1)S(1)} async-done(((bf16[128,32,32]{0,2,1:T(8,128)(2,1)}), bf16[128,32,32]{0,2,1:T(8,128)(2,1)S(1)}, u32[]{:S(2)}, u32[]{:S(2)}) %all-to-all-start.3) | async-done | bytes 262176 | tf_op jit(solution)/shard_map/all_to_all | solution.py:138
  245.1 1.1 reshape.152
  248.0 1.2 fusion.75
  249.2 1.2 fusion.74
  250.4 1.2 convolution_subtract_fusion.5
  252.5 2.0 multiply_subtract_fusion.1
  254.6 1.3 fusion.35
  255.9 1.2 fusion.37
  257.1 1.2 fusion.47
  258.2 1.2 fusion.49
  259.4 1.2 fusion.41
  260.6 1.2 fusion.43
  261.7 1.2 fusion.32
  262.9 1.2 fusion.31
  264.1 1.2 fusion.30
  265.3 1.2 fusion.29
  266.4 1.2 fusion.28
  267.6 3.5 multiply_add_fusion
  271.7 1.6 copy.64
  273.9 1.4 fusion.172
  275.9 1.4 fusion.5
  278.1 1.0 copy.52
  279.1 4.0 all-to-all-start.2
  283.1 1.8 copy.59
  285.6 1.3 fusion.170
  286.9 1.4 fusion.4
  289.1 1.0 copy.61
  290.1 7.6 %all-to-all-done.2 = bf16[32,128,32]{1,2,0:T(8,128)(2,1)S(1)} async-done(((bf16[32,128,32]{1,2,0:T(8,128)(2,1)}), bf16[32,128,32]{1,2,0:T(8,128)(2,1)S(1)}, u32[]{:S(2)}, u32[]{:S(2)}) %all-to-all-start.2) | async-done | bytes 262176 | tf_op jit(solution)/shard_map/all_to_all | solution.py:135
  297.8 4.1 all-to-all-start.4
  301.9 2.6 fusion.168
  304.5 1.4 fusion.3
  306.6 1.0 copy.66
  307.9 8.4 %all-to-all-done.4 = bf16[32,128,32]{1,2,0:T(8,128)(2,1)S(1)} async-done(((bf16[32,128,32]{1,2,0:T(8,128)(2,1)}), bf16[32,128,32]{1,2,0:T(8,128)(2,1)S(1)}, u32[]{:S(2)}, u32[]{:S(2)}) %all-to-all-start.4) | async-done | bytes 262176 | tf_op jit(solution)/shard_map/all_to_all | solution.py:144
  316.3 3.9 all-to-all-start.5
  321.3 1.0 copy-done.8
  322.3 1.7 fusion.25
  324.0 1.3 collective-permute-start.1
  325.4 9.4 %all-to-all-done.5 = bf16[32,128,32]{1,2,0:T(8,128)(2,1)S(1)} async-done(((bf16[32,128,32]{1,2,0:T(8,128)(2,1)}), bf16[32,128,32]{1,2,0:T(8,128)(2,1)S(1)}, u32[]{:S(2)}, u32[]{:S(2)}) %all-to-all-start.5) | async-done | bytes 262176 | tf_op jit(solution)/shard_map/all_to_all | solution.py:145
  334.9 1.0 copy.68
  336.1 2.3 fusion.19
  338.4 236.1 %all-reduce.2.cloned.1.call-done = f32[7,3,1024]{2,1,0:T(4,128)} async-done(((f32[7,3,1024]{2,1,0:T(4,128)}), f32[7,3,1024]{2,1,0:T(4,128)}) %all-reduce.2.cloned.1.call-update) | async-done | bytes 86032 | tf_op jit(solution)/shard_map/psum | solution.py:169
  574.6 1.6 copy.67
  (97 shorter events, 17.6 us)
Async XLA Ops:
  7.2 145.0 %copy-start = (bf16[128,1024]{1,0:T(8,128)(2,1)S(1)}, bf16[128,1024]{1,0:T(8,128)(2,1)}, u32[]{:S(2)}) copy-start(bf16[128,1024]{1,0:T(8,128)(2,1)} %param.6) | copy-start | bytes 786436
  7.2 16.6 %copy-start.21 = (f32[7,3,1024]{2,0,1:T(8,128)S(1)}, f32[7,3,1024]{2,0,1:T(8,128)}, u32[]{:S(2)}) copy-start(f32[7,3,1024]{2,0,1:T(8,128)} %param.8) | copy-start | bytes 258052
  7.2 145.0 %all-gather.2.cloned.1.call-start = ((), (), s32[]{:S(2)}) async-start(), calls=%async_computation.7 | async-start | bytes 17301504 | tf_op jit(solution)/shard_map/all_gather | solution.py:106
  8.7 156.4 %collective-permute-start = (bf16[6,3,1024]{2,0,1:T(8,128)(2,1)S(1)}, bf16[6,3,1024]{2,0,1:T(8,128)(2,1)S(1)}, u32[]{:S(2)}, u32[]{:S(2)}) collective-permute-start(bf16[6,3,1024]{2,0,1:T(8,128)(2,1)S(1)} %slice.87), channel_id=1, source_target_pairs={{0,8},{8,16},{16,24},{24,32},{32,40},{40,48},{48,56},{56,64},{64,7... | collective-permute-start | bytes 110600 | tf_op jit(solution)/shard_map/ppermute | solution.py:13
  12.4 156.1 %all-to-all-start.1 = ((bf16[128,32,32]{0,2,1:T(8,128)(2,1)}), bf16[128,32,32]{0,2,1:T(8,128)(2,1)S(1)}, u32[]{:S(2)}, u32[]{:S(2)}) async-start(bf16[128,32,32]{0,2,1:T(8,128)(2,1)} %bitcast.8), calls=%async_computation.2 | async-start | bytes 524288 | tf_op jit(solution)/shard_map/all_to_all | solution.py:126
  23.7 195.2 %reduce-scatter.2.cloned.1.call-start = ((), (), s32[]{:S(2)}) async-start(), calls=%async_computation.8 | async-start | bytes 2359296 | tf_op jit(solution)/shard_map/reduce_scatter | solution.py:110
  164.9 1.2 copy-start.7
  165.0 3.5 copy-start.11
  165.0 3.5 copy-start.13
  165.0 3.5 copy-start.15
  165.0 3.5 copy-start.17
  165.2 3.3 copy-start.19
  168.5 20.3 %all-to-all-start = ((bf16[128,32,32]{0,2,1:T(8,128)(2,1)}), bf16[128,32,32]{0,2,1:T(8,128)(2,1)S(1)}, u32[]{:S(2)}, u32[]{:S(2)}) async-start(bf16[128,32,32]{0,2,1:T(8,128)(2,1)} %bitcast.2), calls=%async_computation.1 | async-start | bytes 524288 | tf_op jit(solution)/shard_map/all_to_all | solution.py:130
  220.8 23.9 %all-to-all-start.3 = ((bf16[128,32,32]{0,2,1:T(8,128)(2,1)}), bf16[128,32,32]{0,2,1:T(8,128)(2,1)S(1)}, u32[]{:S(2)}, u32[]{:S(2)}) async-start(bf16[128,32,32]{0,2,1:T(8,128)(2,1)} %bitcast.22), calls=%async_computation.4 | async-start | bytes 524288 | tf_op jit(solution)/shard_map/all_to_all | solution.py:138
  250.3 1.2 copy-start.2
  250.4 1.5 copy-start.3
  250.4 1.8 copy-start.4
  250.4 2.1 copy-start.5
  279.1 5.9 %copy-start.6 = (f32[128,64,32]{0,1,2:T(8,128)S(1)}, f32[128,64,32]{0,1,2:T(8,128)}, u32[]{:S(2)}) copy-start(f32[128,64,32]{0,1,2:T(8,128)} %get-tuple-element.48) | copy-start | bytes 3145732
  279.1 18.7 %all-to-all-start.2 = ((bf16[32,128,32]{1,2,0:T(8,128)(2,1)}), bf16[32,128,32]{1,2,0:T(8,128)(2,1)S(1)}, u32[]{:S(2)}, u32[]{:S(2)}) async-start(bf16[32,128,32]{1,2,0:T(8,128)(2,1)} %copy.52), calls=%async_computation.3 | async-start | bytes 524288 | tf_op jit(solution)/shard_map/all_to_all | solution.py:135
  297.8 18.5 %all-to-all-start.4 = ((bf16[32,128,32]{1,2,0:T(8,128)(2,1)}), bf16[32,128,32]{1,2,0:T(8,128)(2,1)S(1)}, u32[]{:S(2)}, u32[]{:S(2)}) async-start(bf16[32,128,32]{1,2,0:T(8,128)(2,1)} %copy.61), calls=%async_computation.5 | async-start | bytes 524288 | tf_op jit(solution)/shard_map/all_to_all | solution.py:144
  316.3 18.5 %all-to-all-start.5 = ((bf16[32,128,32]{1,2,0:T(8,128)(2,1)}), bf16[32,128,32]{1,2,0:T(8,128)(2,1)S(1)}, u32[]{:S(2)}, u32[]{:S(2)}) async-start(bf16[32,128,32]{1,2,0:T(8,128)(2,1)} %copy.66), calls=%async_computation.6 | async-start | bytes 524288 | tf_op jit(solution)/shard_map/all_to_all | solution.py:145
  320.2 1.0 copy-start.9
  320.2 254.4 %all-reduce.2.cloned.1.call-start = ((), (), s32[]{:S(2)}) async-start(), calls=%async_computation.9 | async-start | bytes 229376 | tf_op jit(solution)/shard_map/psum | solution.py:169
  321.1 1.1 copy-start.8
  324.0 11.9 %collective-permute-start.1 = (bf16[6,3,1024]{2,0,1:T(8,128)(2,1)S(1)}, bf16[6,3,1024]{2,0,1:T(8,128)(2,1)S(1)}, u32[]{:S(2)}, u32[]{:S(2)}) collective-permute-start(bf16[6,3,1024]{2,0,1:T(8,128)(2,1)S(1)} %slice.122), channel_id=1, source_target_pairs={{8,0},{16,8},{24,16},{32,24},{40,32},{48,40},{56,48},{64,56},{72,6... | collective-permute-start | bytes 110600 | tf_op jit(solution)/shard_map/ppermute | solution.py:13
  325.4 10.5 %copy-start.10 = (f32[7,3,1024]{2,1,0:T(4,128)}, f32[7,3,1024]{2,1,0:T(4,128)S(1)}, u32[]{:S(2)}) copy-start(f32[7,3,1024]{2,1,0:T(4,128)S(1)} %constant_dynamic-update-slice_fusion) | copy-start | bytes 258052
  334.9 1.2 copy-start.12
  334.9 1.2 copy-start.14
  334.9 1.2 copy-start.16
  334.9 1.2 copy-start.18
  334.9 1.2 copy-start.20
  336.1 240.0 %copy-start.1 = (bf16[128,1024]{1,0:T(8,128)(2,1)S(1)}, bf16[128,1024]{1,0:T(8,128)(2,1)}, u32[]{:S(2)}) copy-start(bf16[128,1024]{1,0:T(8,128)(2,1)} %param.6) | copy-start | bytes 786436
Sparse Core Ops, SparseCore 0:
  10.8 141.3 all-gather.1
  165.1 53.7 reduce-scatter.1
  336.1 238.4 all-reduce.1
where the time goes:
time: 589 us; the launch traced here: 583 us
  waiting for transfers between devices  429 us (73%)
  matrix products  62.1 us (11%)
  starting transfers between devices  41.5 us (7%)
  local copies, waits for them, and re-layouts  27.9 us (5%)
  between operations  15 us (3%)
  other arithmetic  7.24 us (1%)
    psum x1, waiting for transfers between devices, body(): lax.psum(local_short.reshape(-1, channels), 'seq').reshape(short_shape)  236 us
    all_gather x1, waiting for transfers between devices, body(): lax.all_gather(out_weight, 'seq', axis=0, tiled=True)  128 us
    reduce_scatter x1, waiting for transfers between devices, body(): lax.psum_scatter(partial_value.astype(jnp.bfloat16), 'tp', scatter_dimens...  22.9 us
    dot_general x1, matrix products, body(): lax.dot_general(cotangent, lax.all_gather(out_weight, 'seq', axis=0, tile...  12.7 us
  transfers between devices with their start and end apart: 11, of which 8 were waited for; matrix products, arithmetic and copies ran while one was open for 10% of the time, Pallas kernels for 0%

commit v1 on v0

--- a/solution.py
+++ b/solution.py
@@ -166,7 +166,9 @@
         ]
     )
     short_shape = local_short.shape
-    grad_short = lax.psum(local_short.reshape(-1, channels), "seq").reshape(short_shape)
+    grad_short = jnp.sum(lax.all_gather(local_short.reshape(-1, channels), "seq"), axis=0).reshape(
+        short_shape
+    )
     return (grad_proj, grad_short, grad_filter)
 
 

time: 589 us -> 414 us (0.70)
  waiting for transfers between devices: 429 us -> 249 us
    psum x1 -> x0, waiting for transfers between devices: 236 us -> none  [body(): lax.psum(local_short.reshape(-1, channels), 'seq').reshape(short_shape)]
    all_gather x0 -> x1, waiting for transfers between devices: none -> 47.5 us  [body(): lax.all_gather(local_short.reshape(-1, channels), 'seq')]
  transfers between devices with their start and end apart: 11 -> 11, of which waited for: 8 -> 8; matrix products, arithmetic and copies ran while one was open for 10% -> 14% of each run, Pallas kernels for 0% -> 0%
where the time goes in v1:
time: 414 us; the launch traced here: 406 us
  waiting for transfers between devices  249 us (60%)
  matrix products  62.2 us (15%)
  starting transfers between devices  41.2 us (10%)
  local copies, waits for them, and re-layouts  29.2 us (7%)
  between operations  14.9 us (4%)
  other arithmetic  9.58 us (2%)
    all_gather x1, waiting for transfers between devices, body(): lax.all_gather(out_weight, 'seq', axis=0, tiled=True)  128 us
    all_gather x1, waiting for transfers between devices, body(): lax.all_gather(local_short.reshape(-1, channels), 'seq')  47.5 us
    reduce_scatter x1, waiting for transfers between devices, body(): lax.psum_scatter(partial_value.astype(jnp.bfloat16), 'tp', scatter_dimens...  21.1 us
    all_to_all x1, waiting for transfers between devices, body(): lax.all_to_all(filter_grad_cols.astype(jnp.bfloat16), 'seq', split_axis=0...  14 us
    all_to_all x1, waiting for transfers between devices, body(): lax.all_to_all(gated_grad_cols, 'seq', split_axis=0, concat_axis=1, tiled...  13.5 us
    dot_general x1, matrix products, body(): lax.dot_general(cotangent, lax.all_gather(out_weight, 'seq', axis=0, tile...  12.7 us
    all_to_all x1, starting transfers between devices, body(): lax.all_to_all(long_filter.astype(jnp.bfloat16), 'seq', split_axis=1, con...  11.3 us
    all_to_all x1, waiting for transfers between devices, body(): lax.all_to_all(grad_conv, 'seq', split_axis=1, concat_axis=0, tiled=True)  11.3 us
  transfers between devices with their start and end apart: 11, of which 8 were waited for; matrix products, arithmetic and copies ran while one was open for 14% of the time, Pallas kernels for 0%

profile of v1, /device:TPU:2, one launch (start us, length us, event | category | flops | bytes accessed | tf_op | source)
XLA Modules:
  0.0 405.7 jit_solution(17451014721823698917)
XLA Ops:
  8.7 1.7 collective-permute-start
  10.5 1.9 copy.45
  12.4 11.3 %all-to-all-start.1 = ((bf16[128,32,32]{0,2,1:T(8,128)(2,1)}), bf16[128,32,32]{0,2,1:T(8,128)(2,1)S(1)}, u32[]{:S(2)}, u32[]{:S(2)}) async-start(bf16[128,32,32]{0,2,1:T(8,128)(2,1)} %bitcast.8), calls=%async_computation.2 | async-start | bytes 524288 | tf_op jit(solution)/shard_map/all_to_all | solution.py:126
  23.9 128.3 %all-gather.3.cloned.1.call-done = bf16[8192,1024]{1,0:T(8,128)(2,1)} async-done(((bf16[256,1024]{1,0:T(8,128)(2,1)}), bf16[8192,1024]{1,0:T(8,128)(2,1)}) %all-gather.3.cloned.1.call-update) | async-done | bytes 16777232 | tf_op jit(solution)/shard_map/all_gather | solution.py:106
  152.2 12.7 %convolution_convert_fusion = bf16[128,8192]{1,0:T(8,128)(2,1)} fusion(bf16[128,1024]{1,0:T(8,128)(2,1)S(1)} %copy-done, bf16[8192,1024]{1,0:T(8,128)(2,1)} %all-gather.3.cloned.1.call-done), kind=kOutput, calls=%fused_computation | convolution fusion | flops 2148532224 | bytes 19136512 | tf_op jit(solution)/shard_map/dot_general | solution.py:104
  166.1 1.5 fusion.12
  168.5 5.8 %all-to-all-start = ((bf16[128,32,32]{0,2,1:T(8,128)(2,1)}), bf16[128,32,32]{0,2,1:T(8,128)(2,1)S(1)}, u32[]{:S(2)}, u32[]{:S(2)}) async-start(bf16[128,32,32]{0,2,1:T(8,128)(2,1)} %bitcast.2), calls=%async_computation.1 | async-start | bytes 524288 | tf_op jit(solution)/shard_map/all_to_all | solution.py:130
  174.8 1.1 reshape.146
  177.6 1.2 fusion.73
  178.8 2.1 convolution_subtract_fusion.7
  181.0 1.2 fusion.72
  182.1 2.1 convolution_add_fusion.4
  184.3 4.5 %all-to-all-done = bf16[128,32,32]{0,2,1:T(8,128)(2,1)S(1)} async-done(((bf16[128,32,32]{0,2,1:T(8,128)(2,1)}), bf16[128,32,32]{0,2,1:T(8,128)(2,1)S(1)}, u32[]{:S(2)}, u32[]{:S(2)}) %all-to-all-start) | async-done | bytes 262176 | tf_op jit(solution)/shard_map/all_to_all | solution.py:130
  189.3 1.1 reshape.145
  192.2 1.8 fusion.68
  194.0 1.6 fusion.71
  195.6 2.2 convolution_subtract_fusion.8
  197.8 21.1 %reduce-scatter.2.cloned.1.call-done = bf16[128,1024]{1,0:T(8,128)(2,1)} async-done(((bf16[128,8192]{1,0:T(8,128)(2,1)}), bf16[128,1024]{1,0:T(8,128)(2,1)}) %reduce-scatter.2.cloned.1.call-update) | async-done | bytes 262160 | tf_op jit(solution)/shard_map/reduce_scatter | solution.py:110
  218.9 1.0 fusion.57
  220.8 9.2 %all-to-all-start.3 = ((bf16[128,32,32]{0,2,1:T(8,128)(2,1)}), bf16[128,32,32]{0,2,1:T(8,128)(2,1)S(1)}, u32[]{:S(2)}, u32[]{:S(2)}) async-start(bf16[128,32,32]{0,2,1:T(8,128)(2,1)} %bitcast.204), calls=%async_computation.4 | async-start | bytes 524288 | tf_op jit(solution)/shard_map/all_to_all | solution.py:138
  230.0 1.2 fusion.70
  231.2 2.2 convolution_add_fusion.5
  233.3 11.3 %all-to-all-done.3 = bf16[128,32,32]{0,2,1:T(8,128)(2,1)S(1)} async-done(((bf16[128,32,32]{0,2,1:T(8,128)(2,1)}), bf16[128,32,32]{0,2,1:T(8,128)(2,1)S(1)}, u32[]{:S(2)}, u32[]{:S(2)}) %all-to-all-start.3) | async-done | bytes 262176 | tf_op jit(solution)/shard_map/all_to_all | solution.py:138
  245.1 1.1 reshape.149
  248.0 1.2 fusion.75
  249.2 1.2 fusion.74
  250.4 1.2 convolution_subtract_fusion.5
  252.5 2.0 multiply_subtract_fusion.1
  254.6 1.3 fusion.35
  255.9 1.2 fusion.37
  257.1 1.2 fusion.47
  258.2 1.2 fusion.49
  259.4 1.2 fusion.41
  260.6 1.2 fusion.43
  261.7 1.2 fusion.32
  262.9 1.2 fusion.31
  264.1 1.2 fusion.30
  265.3 1.2 fusion.29
  266.4 1.2 fusion.28
  267.6 3.6 multiply_add_fusion
  271.8 1.4 fusion.172
  273.8 1.4 fusion.5
  276.0 1.0 copy.52
  277.0 4.0 all-to-all-start.2
  281.0 1.8 copy.59
  283.5 1.4 fusion.170
  284.9 1.4 fusion.4
  287.1 1.0 copy.61
  288.1 7.6 %all-to-all-done.2 = bf16[32,128,32]{1,2,0:T(8,128)(2,1)S(1)} async-done(((bf16[32,128,32]{1,2,0:T(8,128)(2,1)}), bf16[32,128,32]{1,2,0:T(8,128)(2,1)S(1)}, u32[]{:S(2)}, u32[]{:S(2)}) %all-to-all-start.2) | async-done | bytes 262176 | tf_op jit(solution)/shard_map/all_to_all | solution.py:135
  295.7 3.9 all-to-all-start.4
  299.7 1.0 copy.53
  300.7 13.5 %all-to-all-done.4 = bf16[32,128,32]{1,2,0:T(8,128)(2,1)S(1)} async-done(((bf16[32,128,32]{1,2,0:T(8,128)(2,1)}), bf16[32,128,32]{1,2,0:T(8,128)(2,1)S(1)}, u32[]{:S(2)}, u32[]{:S(2)}) %all-to-all-start.4) | async-done | bytes 262176 | tf_op jit(solution)/shard_map/all_to_all | solution.py:144
  315.8 2.0 fusion.25
  318.6 1.8 copy.65
  321.1 1.3 fusion.168
  322.4 1.4 fusion.3
  324.6 1.0 copy.66
  325.6 3.9 all-to-all-start.5
  329.6 1.3 collective-permute-start.1
  330.9 14.0 %all-to-all-done.5 = bf16[32,128,32]{1,2,0:T(8,128)(2,1)S(1)} async-done(((bf16[32,128,32]{1,2,0:T(8,128)(2,1)}), bf16[32,128,32]{1,2,0:T(8,128)(2,1)S(1)}, u32[]{:S(2)}, u32[]{:S(2)}) %all-to-all-start.5) | async-done | bytes 262176 | tf_op jit(solution)/shard_map/all_to_all | solution.py:145
  345.0 1.0 copy.68
  346.1 2.3 fusion.19
  348.4 47.5 %all-gather.5.cloned.1.call-done = f32[32,21,1024]{2,1,0:T(8,128)} async-done(((f32[1,21,1024]{2,1,0:T(8,128)}), f32[32,21,1024]{2,1,0:T(8,128)}) %all-gather.5.cloned.1.call-update) | async-done | bytes 2752528 | tf_op jit(solution)/shard_map/all_gather | solution.py:169
  395.9 2.1 reduce_sum.79
  (86 shorter events, 20.4 us)
Async XLA Ops:
  7.2 145.0 %copy-start = (bf16[128,1024]{1,0:T(8,128)(2,1)S(1)}, bf16[128,1024]{1,0:T(8,128)(2,1)}, u32[]{:S(2)}) copy-start(bf16[128,1024]{1,0:T(8,128)(2,1)} %param.6) | copy-start | bytes 786436
  7.2 16.6 %copy-start.14 = (f32[7,3,1024]{2,0,1:T(8,128)S(1)}, f32[7,3,1024]{2,0,1:T(8,128)}, u32[]{:S(2)}) copy-start(f32[7,3,1024]{2,0,1:T(8,128)} %param.8) | copy-start | bytes 258052
  7.2 145.0 %all-gather.3.cloned.1.call-start = ((), (), s32[]{:S(2)}) async-start(), calls=%async_computation.7 | async-start | bytes 17301504 | tf_op jit(solution)/shard_map/all_gather | solution.py:106
  8.7 156.4 %collective-permute-start = (bf16[6,3,1024]{2,0,1:T(8,128)(2,1)S(1)}, bf16[6,3,1024]{2,0,1:T(8,128)(2,1)S(1)}, u32[]{:S(2)}, u32[]{:S(2)}) collective-permute-start(bf16[6,3,1024]{2,0,1:T(8,128)(2,1)S(1)} %slice.87), channel_id=1, source_target_pairs={{0,8},{8,16},{16,24},{24,32},{32,40},{40,48},{48,56},{56,64},{64,7... | collective-permute-start | bytes 110600 | tf_op jit(solution)/shard_map/ppermute | solution.py:13
  12.4 156.1 %all-to-all-start.1 = ((bf16[128,32,32]{0,2,1:T(8,128)(2,1)}), bf16[128,32,32]{0,2,1:T(8,128)(2,1)S(1)}, u32[]{:S(2)}, u32[]{:S(2)}) async-start(bf16[128,32,32]{0,2,1:T(8,128)(2,1)} %bitcast.8), calls=%async_computation.2 | async-start | bytes 524288 | tf_op jit(solution)/shard_map/all_to_all | solution.py:126
  23.7 195.2 %reduce-scatter.2.cloned.1.call-start = ((), (), s32[]{:S(2)}) async-start(), calls=%async_computation.8 | async-start | bytes 2359296 | tf_op jit(solution)/shard_map/reduce_scatter | solution.py:110
  164.9 1.1 copy-start.8
  165.1 3.3 copy-start.12
  168.5 20.3 %all-to-all-start = ((bf16[128,32,32]{0,2,1:T(8,128)(2,1)}), bf16[128,32,32]{0,2,1:T(8,128)(2,1)S(1)}, u32[]{:S(2)}, u32[]{:S(2)}) async-start(bf16[128,32,32]{0,2,1:T(8,128)(2,1)} %bitcast.2), calls=%async_computation.1 | async-start | bytes 524288 | tf_op jit(solution)/shard_map/all_to_all | solution.py:130
  190.7 0.8 copy-start.2
  220.8 23.9 %all-to-all-start.3 = ((bf16[128,32,32]{0,2,1:T(8,128)(2,1)}), bf16[128,32,32]{0,2,1:T(8,128)(2,1)S(1)}, u32[]{:S(2)}, u32[]{:S(2)}) async-start(bf16[128,32,32]{0,2,1:T(8,128)(2,1)} %bitcast.204), calls=%async_computation.4 | async-start | bytes 524288 | tf_op jit(solution)/shard_map/all_to_all | solution.py:138
  250.3 1.2 copy-start.3
  250.3 1.5 copy-start.4
  250.4 1.8 copy-start.5
  250.4 2.1 copy-start.6
  277.0 5.9 %copy-start.7 = (f32[128,64,32]{0,1,2:T(8,128)S(1)}, f32[128,64,32]{0,1,2:T(8,128)}, u32[]{:S(2)}) copy-start(f32[128,64,32]{0,1,2:T(8,128)} %get-tuple-element.48) | copy-start | bytes 3145732
  277.0 18.7 %all-to-all-start.2 = ((bf16[32,128,32]{1,2,0:T(8,128)(2,1)}), bf16[32,128,32]{1,2,0:T(8,128)(2,1)S(1)}, u32[]{:S(2)}, u32[]{:S(2)}) async-start(bf16[32,128,32]{1,2,0:T(8,128)(2,1)} %copy.52), calls=%async_computation.3 | async-start | bytes 524288 | tf_op jit(solution)/shard_map/all_to_all | solution.py:135
  295.7 18.5 %all-to-all-start.4 = ((bf16[32,128,32]{1,2,0:T(8,128)(2,1)}), bf16[32,128,32]{1,2,0:T(8,128)(2,1)S(1)}, u32[]{:S(2)}, u32[]{:S(2)}) async-start(bf16[32,128,32]{1,2,0:T(8,128)(2,1)} %copy.61), calls=%async_computation.5 | async-start | bytes 524288 | tf_op jit(solution)/shard_map/all_to_all | solution.py:144
  299.6 96.3 %all-gather.5.cloned.1.call-start = ((), (), s32[]{:S(2)}) async-start(), calls=%async_computation.9 | async-start | bytes 3244032 | tf_op jit(solution)/shard_map/all_gather | solution.py:169
  300.7 14.0 %copy-start.11 = (bf16[128,1024]{1,0:T(8,128)(2,1)S(1)}, bf16[128,1024]{1,0:T(8,128)(2,1)}, u32[]{:S(2)}) copy-start(bf16[128,1024]{1,0:T(8,128)(2,1)} %reduce-scatter.2.cloned.1.call-done) | copy-start | bytes 786436
  314.5 1.0 copy-start.10
  314.5 1.3 copy-start.9
  325.6 19.3 %all-to-all-start.5 = ((bf16[32,128,32]{1,2,0:T(8,128)(2,1)}), bf16[32,128,32]{1,2,0:T(8,128)(2,1)S(1)}, u32[]{:S(2)}, u32[]{:S(2)}) async-start(bf16[32,128,32]{1,2,0:T(8,128)(2,1)} %copy.66), calls=%async_computation.6 | async-start | bytes 524288 | tf_op jit(solution)/shard_map/all_to_all | solution.py:145
  329.6 16.5 %copy-start.13 = (f32[1,3,1024]{2,1,0:T(4,128)S(1)}, f32[1,3,1024]{2,1,0:T(4,128)}, u32[]{:S(2)}) copy-start(f32[1,3,1024]{2,1,0:T(4,128)} %copy-done.12) | copy-start | bytes 36868
  329.6 16.4 %collective-permute-start.1 = (bf16[6,3,1024]{2,0,1:T(8,128)(2,1)S(1)}, bf16[6,3,1024]{2,0,1:T(8,128)(2,1)S(1)}, u32[]{:S(2)}, u32[]{:S(2)}) collective-permute-start(bf16[6,3,1024]{2,0,1:T(8,128)(2,1)S(1)} %slice.122), channel_id=1, source_target_pairs={{8,0},{16,8},{24,16},{32,24},{40,32},{48,40},{56,48},{64,56},{72,6... | collective-permute-start | bytes 110600 | tf_op jit(solution)/shard_map/ppermute | solution.py:13
  346.1 52.6 %copy-start.1 = (bf16[128,1024]{1,0:T(8,128)(2,1)S(1)}, bf16[128,1024]{1,0:T(8,128)(2,1)}, u32[]{:S(2)}) copy-start(bf16[128,1024]{1,0:T(8,128)(2,1)} %param.6) | copy-start | bytes 786436
Sparse Core Ops, SparseCore 0:
  10.8 141.3 all-gather.2
  165.1 53.7 reduce-scatter.1
  318.7 77.0 all-gather.4
